TPU v7x, 256 devices: a whole 4x4x8 slice. The times are simulated.
256 devices in a mesh: dp: 4 (over x), node: 2 (over core), local: 32 (over z, y).
Axes of the slice: x: 4, y: 4, z: 8, core: 2. Of those that a mesh axis runs over, the one named last changes fastest.
Arguments:
- tokens: bfloat16 [32768, 2048], P(('dp', 'node', 'local')), may hold values from -6 to 6
- cotangent: bfloat16 [32768, 2048], P(('dp', 'node', 'local')), may hold values from -4 to 4
- routes: int32 [32768, 8], P(('dp', 'node', 'local')), may hold values from 0 to 63, all different within a row; in each aligned block of 128 rows (0 to 127, 128 to 255, ...) at most 24 rows name the same one
- gates: bfloat16 [32768, 8], P(('dp', 'node', 'local')), may hold values from 0.029907227 to 0.3984375
- w_gate: bfloat16 [64, 2048, 384], P(('node', 'local'), 'dp'), may hold values from -0.125 to 0.125
- w_up: bfloat16 [64, 2048, 384], P(('node', 'local'), 'dp'), may hold values from -0.125 to 0.125
- w_down: bfloat16 [64, 2048, 384], P(('node', 'local'), 'dp'), may hold values from -0.3125 to 0.3125
Outputs:
- input_grad: bfloat16 [32768, 2048], P(('dp', 'node', 'local'))
- gate_grad: bfloat16 [32768, 8], P(('dp', 'node', 'local'))
- gate_weight_grad: float32 [64, 2048, 384], P(('node', 'local'), 'dp')
- up_weight_grad: float32 [64, 2048, 384], P(('node', 'local'), 'dp')
- down_weight_grad: float32 [64, 2048, 384], P(('node', 'local'), 'dp')
Inputs may be any that keep to these rules, and one draw needn't show every extreme that they name: `routes`: each token names 8 different experts. Among the tokens of one device no expert is named more than 24 times, and on some device some expert is named exactly 24 times.
All inputs are finite; a program needn't handle non-finite values.
Results may differ from a plain program's by a relative error of at most 0.0057.
Values may be sent and summed in bfloat16 or wider, within the bound.
No kernel may reach another device: no remote copies, remote signals or barrier semaphores. Data moves between devices by JAX's collectives and lax.ppermute only.
A program may use at most 128 MiB of HBM per device.

v0:
```python
import jax
import jax.numpy as jnp
from jax import lax
from jax.sharding import PartitionSpec as P


def expert_rows(rows_x, rows_dy, rows_gate, gate_proj, up_proj, down_proj):
    pre_gate = jnp.dot(rows_x, gate_proj, preferred_element_type=jnp.float32)
    pre_up = jnp.dot(rows_x, up_proj, preferred_element_type=jnp.float32)
    gate_sigmoid = jax.nn.sigmoid(pre_gate)
    activated = pre_gate * gate_sigmoid
    hidden = activated * pre_up
    upstream = jnp.dot(rows_dy, down_proj, preferred_element_type=jnp.float32)
    gate_grad = jnp.sum(upstream * hidden, axis=1).astype(jnp.bfloat16)
    weight = rows_gate.astype(jnp.float32)[:, None]
    scaled_hidden = (weight * hidden).astype(jnp.bfloat16)
    hidden_grad = weight * upstream
    pre_gate_grad = (
        hidden_grad * pre_up * gate_sigmoid * (1.0 + pre_gate * (1.0 - gate_sigmoid))
    ).astype(jnp.bfloat16)
    pre_up_grad = (hidden_grad * activated).astype(jnp.bfloat16)
    over_rows = (((0,), (0,)), ((), ()))
    down_grad = lax.dot_general(
        rows_dy, scaled_hidden, over_rows, preferred_element_type=jnp.float32
    )
    gate_wgrad = lax.dot_general(
        rows_x, pre_gate_grad, over_rows, preferred_element_type=jnp.float32
    )
    up_wgrad = lax.dot_general(rows_x, pre_up_grad, over_rows, preferred_element_type=jnp.float32)
    over_hidden = (((1,), (1,)), ((), ()))
    input_rows = lax.dot_general(
        pre_gate_grad, gate_proj, over_hidden, preferred_element_type=jnp.float32
    )
    input_rows = input_rows + lax.dot_general(
        pre_up_grad, up_proj, over_hidden, preferred_element_type=jnp.float32
    )
    return (input_rows.astype(jnp.bfloat16), gate_grad, gate_wgrad, up_wgrad, down_grad)


def local(tokens, cotangent, routes, gates, w_gate, w_up, w_down):
    tokens_dev, top_count = routes.shape
    width = tokens.shape[1]
    hidden_units = w_gate.shape[2]
    cores = lax.axis_size("node")
    planes = lax.axis_size("lz")
    rows_of = lax.axis_size("ly")
    experts = cores * planes * rows_of
    capacity = min(
        tokens_dev,
        max(3 * tokens_dev * top_count // (2 * experts), tokens_dev * top_count // experts),
    )
    near = cores * rows_of
    slots = near * planes * capacity
    half = width // 2
    meta = jnp.concatenate([gates, routes.astype(jnp.bfloat16)], axis=1).reshape(1, -1)
    meta = jnp.pad(meta, ((0, 0), (0, width - meta.shape[1])))
    seen_row = lax.all_gather(meta, "lz", axis=0, tiled=False)
    seen_x = lax.all_gather(tokens, "lz", axis=0, tiled=False)
    seen_dy = lax.all_gather(cotangent, "lz", axis=0, tiled=False)
    seen_meta = seen_row[:, 0, : 2 * tokens_dev * top_count].reshape(
        planes, tokens_dev, 2 * top_count
    )
    seen_gates = seen_meta[..., :top_count]
    seen_routes = seen_meta[..., top_count:].astype(jnp.int32)
    plane = lax.axis_index("lz")
    near_ids = jnp.arange(near, dtype=jnp.int32)
    near_experts = near_ids // rows_of * (planes * rows_of) + plane * rows_of + near_ids % rows_of
    hit = seen_routes[..., None] == near_experts
    named = jnp.any(hit, axis=2)
    earlier = (jnp.arange(tokens_dev)[:, None] > jnp.arange(tokens_dev)[None, :]).astype(
        jnp.bfloat16
    )
    rank = jnp.einsum(
        "ts,zsj->jzt", earlier, named.astype(jnp.bfloat16), preferred_element_type=jnp.float32
    ).astype(jnp.int32)
    choose = jnp.transpose(named, (2, 0, 1))[:, :, None, :] & (
        rank[:, :, None, :] == jnp.arange(capacity, dtype=jnp.int32)[None, None, :, None]
    )
    choose_b = choose.astype(jnp.bfloat16)
    gate_tj = jnp.sum(jnp.where(hit, seen_gates[..., None], jnp.zeros((), jnp.bfloat16)), axis=2)
    send_gate = jnp.sum(
        jnp.where(
            choose, jnp.transpose(gate_tj, (2, 0, 1))[:, :, None, :], jnp.zeros((), jnp.bfloat16)
        ),
        axis=3,
    )
    gate_row = jnp.pad(
        send_gate.reshape(near, 1, planes * capacity),
        ((0, 0), (0, 0), (0, width - planes * capacity)),
    )
    send_x = jnp.einsum(
        "jzrt,ztd->jzrd", choose_b, seen_x, preferred_element_type=jnp.float32
    ).astype(jnp.bfloat16)
    send_x = jnp.concatenate([send_x.reshape(near, planes * capacity, width), gate_row], axis=1)
    send_dy = (
        jnp.einsum("jzrt,ztd->jzrd", choose_b, seen_dy, preferred_element_type=jnp.float32)
        .astype(jnp.bfloat16)
        .reshape(near, planes * capacity, width)
    )
    all_weights = lax.all_gather(
        jnp.concatenate([w_gate, w_up, w_down], axis=2), "dp", axis=1, tiled=True
    )[0]
    gate_proj = all_weights[:, :hidden_units]
    up_proj = all_weights[:, hidden_units : 2 * hidden_units]
    down_proj = all_weights[:, 2 * hidden_units :]
    recv_x = lax.all_to_all(send_x, ("node", "ly"), split_axis=0, concat_axis=0, tiled=True)
    recv_dy = lax.all_to_all(send_dy, ("node", "ly"), split_axis=0, concat_axis=0, tiled=True)
    results = expert_rows(
        recv_x[:, : planes * capacity, :].reshape(slots, width),
        recv_dy.reshape(slots, width),
        recv_x[:, planes * capacity, : planes * capacity].reshape(slots),
        gate_proj,
        up_proj,
        down_proj,
    )
    grad_row = jnp.pad(
        results[1].reshape(near, 1, planes * capacity),
        ((0, 0), (0, 0), (0, half - planes * capacity)),
    )
    back_lo = jnp.concatenate(
        [results[0][:, :half].reshape(near, planes * capacity, half), grad_row], axis=1
    )
    back_hi = results[0][:, half:].reshape(near, planes * capacity, width - half)
    home_lo = lax.all_to_all(back_lo, ("node", "ly"), split_axis=0, concat_axis=0, tiled=True)
    home_gate = home_lo[:, planes * capacity, : planes * capacity].reshape(near, planes, capacity)
    home_lo = home_lo[:, : planes * capacity, :].reshape(near, planes, capacity, half)
    home_hi = lax.all_to_all(
        back_hi, ("node", "ly"), split_axis=0, concat_axis=0, tiled=True
    ).reshape(near, planes, capacity, width - half)
    partial_lo = jnp.einsum("jzrt,jzrd->ztd", choose_b, home_lo, preferred_element_type=jnp.float32)
    gate_jzt = jnp.sum(jnp.where(choose, home_gate[..., None], jnp.zeros((), jnp.bfloat16)), axis=2)
    pick_gate = jnp.sum(
        jnp.where(
            hit, jnp.transpose(gate_jzt, (1, 2, 0))[:, :, None, :], jnp.zeros((), jnp.bfloat16)
        ),
        axis=3,
    )
    gate_cols = jnp.pad(
        pick_gate.astype(jnp.float32).reshape(planes, 1, tokens_dev * top_count),
        ((0, 0), (0, 0), (0, half - tokens_dev * top_count)),
    )
    summed_down = lax.psum_scatter(results[4], "dp", scatter_dimension=0, tiled=True)
    summed = lax.psum_scatter(
        jnp.concatenate([results[2], results[3]], axis=1), "dp", scatter_dimension=0, tiled=True
    )
    summed_down, summed, partial_lo, gate_cols = lax.optimization_barrier(
        (summed_down, summed, partial_lo, gate_cols)
    )
    reduced_lo = lax.psum_scatter(
        jnp.concatenate([partial_lo, gate_cols], axis=1), "lz", scatter_dimension=0, tiled=True
    )[0]
    partial_hi = jnp.einsum("jzrt,jzrd->ztd", choose_b, home_hi, preferred_element_type=jnp.float32)
    reduced_hi = lax.psum_scatter(partial_hi, "lz", scatter_dimension=0, tiled=True)[0]
    input_grad = jnp.concatenate([reduced_lo[:tokens_dev], reduced_hi], axis=1).astype(jnp.bfloat16)
    gate_grad = (
        reduced_lo[tokens_dev, : tokens_dev * top_count]
        .reshape(tokens_dev, top_count)
        .astype(jnp.bfloat16)
    )
    return (
        input_grad,
        gate_grad,
        summed[None, :, :hidden_units],
        summed[None, :, hidden_units : 2 * hidden_units],
        summed_down[None],
    )


def solution(mesh):
    local_size = mesh.shape["local"]
    rows_of = 4 if local_size % 4 == 0 else 1
    split = jax.sharding.Mesh(
        mesh.devices.reshape(mesh.shape["dp"], mesh.shape["node"], local_size // rows_of, rows_of),
        ("dp", "node", "lz", "ly"),
    )
    rows = P(("dp", "node", "lz", "ly"), None)
    expert = P(("node", "lz", "ly"), "dp", None)
    return jax.shard_map(
        local,
        mesh=split,
        in_specs=(rows, rows, rows, rows, expert, expert, expert),
        out_specs=(rows, rows, expert, expert, expert),
        check_vma=False,
    )
```

profile of v0, /device:TPU:1, one launch (start us, length us, event | category | flops | bytes accessed | tf_op | source)
XLA Modules:
  0.0 475.3 jit_solution(9930952564812045546)
XLA Ops:
  10.3 23.4 %all_gather.22 = bf16[8,1,2048]{2,1,0:T(2,128)(2,1)S(1)} all-gather(bf16[1,1,2048]{2,1,0:T(2,128)(2,1)S(1)} %all_gather.21), channel_id=1, replica_groups=mesh['dp'=4,'node'=2,'lz'=8,'ly'=4] {'lz'}, dimensions={0}, use_global_device_ids=true | all-gather | bytes 36864 | tf_op jit(solution)/shard_map/all_gather | solution.py:57
  35.3 33.4 %all-gather.10.cloned.1.call-done = bf16[1024,2048]{1,0:T(8,128)(2,1)} async-done(((bf16[128,2048]{1,0:T(8,128)(2,1)}), bf16[1024,2048]{1,0:T(8,128)(2,1)}) %all-gather.10.cloned.1.call-update) | async-done | bytes 4194320 | tf_op jit(solution)/shard_map/all_gather | solution.py:58
  68.7 4.0 convert_bitcast_fusion
  73.8 3.3 fusion.1
  77.1 5.5 %all-to-all-start.1 = ((bf16[8,193,2048]{2,1,0:T(8,128)(2,1)}), bf16[8,193,2048]{2,1,0:T(8,128)(2,1)}, u32[]{:S(2)}, u32[]{:S(2)}) async-start(bf16[8,193,2048]{2,1,0:T(8,128)(2,1)} %fusion.1), calls=%async_computation.1 | async-start | bytes 13107200 | tf_op jit(solution)/shard_map/all_to_all | solution.py:106
  83.8 40.2 %all-gather.8.cloned.1.call-done = bf16[1024,2048]{1,0:T(8,128)(2,1)} async-done(((bf16[128,2048]{1,0:T(8,128)(2,1)}), bf16[1024,2048]{1,0:T(8,128)(2,1)}) %all-gather.8.cloned.1.call-update) | async-done | bytes 4194320 | tf_op jit(solution)/shard_map/all_gather | solution.py:59
  123.9 4.0 convert_bitcast_fusion.1
  127.9 3.2 copy.60
  131.1 25.9 %all-to-all-done.1 = bf16[8,193,2048]{2,1,0:T(8,128)(2,1)} async-done(((bf16[8,193,2048]{2,1,0:T(8,128)(2,1)}), bf16[8,193,2048]{2,1,0:T(8,128)(2,1)}, u32[]{:S(2)}, u32[]{:S(2)}) %all-to-all-start.1) | async-done | bytes 6324256 | tf_op jit(solution)/shard_map/all_to_all | solution.py:106
  157.0 4.8 %all-to-all-start = ((bf16[8,192,2048]{2,1,0:T(8,128)(2,1)}), bf16[8,192,2048]{2,1,0:T(8,128)(2,1)}, u32[]{:S(2)}, u32[]{:S(2)}) async-start(bf16[8,192,2048]{2,1,0:T(8,128)(2,1)} %bitcast.59), calls=%async_computation | async-start | bytes 12582912 | tf_op jit(solution)/shard_map/all_to_all | solution.py:107
  162.8 6.6 %slice.70 = bf16[8,192,2048]{2,1,0:T(8,128)(2,1)} slice(bf16[8,193,2048]{2,1,0:T(8,128)(2,1)} %all-to-all-done.1), slice={[0:8], [0:192], [0:2048]} | slice | bytes 12582912 | tf_op jit(solution)/shard_map/slice | solution.py:109
  169.4 10.1 %all-gather.6.cloned.1.call-done = bf16[1,2048,1152]{2,1,0:T(8,128)(2,1)} async-done(((bf16[1,512,1152]{2,1,0:T(8,128)(2,1)}), bf16[1,2048,1152]{2,1,0:T(8,128)(2,1)}) %all-gather.6.cloned.1.call-update) | async-done | bytes 4718608 | tf_op jit(solution)/shard_map/all_gather | solution.py:100
  179.6 7.4 %fusion.18 = f32[1536,384]{0,1:T(8,128)} fusion(bf16[1536,2048]{1,0:T(8,128)(2,1)} %bitcast.67, bf16[2048,1152]{1,0:T(8,128)(2,1)} %bitcast.71), kind=kOutput, calls=%fused_computation.26 | convolution fusion | flops 2415919104 | bytes 10223616 | tf_op jit(solution)/shard_map/dot_general | solution.py:9
  187.0 5.5 %fusion.22 = f32[1536,384]{0,1:T(8,128)} fusion(bf16[1536,2048]{1,0:T(8,128)(2,1)S(1)} %bitcast.70, bf16[2048,1152]{1,0:T(8,128)(2,1)} %bitcast.72), kind=kOutput, calls=%fused_computation.30 | convolution fusion | flops 2415919104 | bytes 10223616 | tf_op jit(solution)/shard_map/dot_general | solution.py:8
  192.5 40.5 %all-to-all-done = bf16[8,192,2048]{2,1,0:T(8,128)(2,1)} async-done(((bf16[8,192,2048]{2,1,0:T(8,128)(2,1)}), bf16[8,192,2048]{2,1,0:T(8,128)(2,1)}, u32[]{:S(2)}, u32[]{:S(2)}) %all-to-all-start) | async-done | bytes 6291488 | tf_op jit(solution)/shard_map/all_to_all | solution.py:107
  233.0 9.4 %fusion.24 = f32[2048,384]{1,0:T(8,128)} fusion(bf16[1536,2048]{1,0:T(8,128)(2,1)} %bitcast.8, f32[1536]{0:T(1024)S(1)} %reshape.115, f32[1536,384]{0,1:T(8,128)} %fusion.18, f32[1536,384]{0,1:T(8,128)} %fusion.22), kind=kOutput, calls=%fused_computation.32 | convolution fusion | flops 2420047872 | bytes 14161920 | tf_op jit(solution)/shard_map/dot_general | solution.py:23
  242.8 8.4 %multiply_reduce_fusion = (bf16[1536]{0:T(1024)(128)(2,1)S(1)}, bf16[1536,384]{0,1:T(8,128)(2,1)S(1)}, bf16[1536,384]{0,1:T(8,128)(2,1)S(1)}) fusion(f32[1536,384]{0,1:T(8,128)} %fusion.18, f32[1536,384]{0,1:T(8,128)} %fusion.22, f32[1536]{0:T(1024)S(1)} %reshape.115, bf16[1536,2048]{1,0:T(8,128)(2,1)} %bitcast.8, bf16[2048,1152]{1,0:T(8,128)(2,1)} %bitcast.73), kind=kOutput, calls=%fused_computation.15 | convolution fusion | flops 2425944576 | bytes 14951424 | tf_op jit(solution)/shard_map/dot_general | solution.py:13
  251.2 5.2 %fusion.56 = f32[2048,384]{0,1:T(8,128)S(1)} fusion(bf16[1536,384]{0,1:T(8,128)(2,1)S(1)} %get-tuple-element.39, bf16[1536,2048]{1,0:T(8,128)(2,1)} %bitcast.68), kind=kOutput, calls=%fused_computation.79 | convolution fusion | flops 2415919104 | bytes 10616832 | tf_op jit(solution)/shard_map/dot_general | solution.py:26
  256.3 4.8 %fusion.57 = f32[2048,384]{0,1:T(8,128)S(1)} fusion(bf16[1536,384]{0,1:T(8,128)(2,1)S(1)} %get-tuple-element.42, bf16[1536,2048]{1,0:T(8,128)(2,1)} %bitcast.69), kind=kOutput, calls=%fused_computation.80 | convolution fusion | flops 2415919104 | bytes 10616832 | tf_op jit(solution)/shard_map/dot_general | solution.py:29
  261.1 3.1 pad_maximum_fusion
  264.5 4.9 %fusion.20 = f32[1536,2048]{1,0:T(8,128)S(1)} fusion(bf16[1536,384]{0,1:T(8,128)(2,1)S(1)} %get-tuple-element.39, bf16[2048,1152]{1,0:T(8,128)(2,1)} %bitcast.74), kind=kOutput, calls=%fused_computation.28 | convolution fusion | flops 2415919104 | bytes 15335424 | tf_op jit(solution)/shard_map/dot_general | solution.py:31
  269.4 5.5 %add_convert_fusion = bf16[1536,2048]{1,0:T(8,128)(2,1)S(1)} fusion(f32[1536,2048]{1,0:T(8,128)S(1)} %fusion.20, bf16[1536,384]{0,1:T(8,128)(2,1)} %copy-done.3, bf16[2048,1152]{1,0:T(8,128)(2,1)} %bitcast.75), kind=kOutput, calls=%fused_computation.2 | convolution fusion | flops 2422210560 | bytes 21626880 | tf_op jit(solution)/shard_map/dot_general | solution.py:34
  274.9 2.5 fusion.54
  277.3 41.4 %all_to_all.20 = bf16[8,192,1024]{2,1,0:T(8,128)(2,1)S(1)} all-to-all(bf16[8,192,1024]{2,1,0:T(8,128)(2,1)S(1)} %bitcast.64), channel_id=1, replica_groups=mesh['dp'=4,'node'=2,'lz'=8,'ly'=4] {'node','ly'}, dimensions={0} | all-to-all | bytes 6291456 | tf_op jit(solution)/shard_map/all_to_all | solution.py:127
  318.7 2.8 fusion.12
  321.7 1.7 copy-done
  323.8 41.8 %all_to_all.21 = bf16[8,193,1024]{2,1,0:T(8,128)(2,1)S(1)} all-to-all(bf16[8,193,1024]{2,1,0:T(8,128)(2,1)S(1)} %fusion.3), channel_id=1, replica_groups=mesh['dp'=4,'node'=2,'lz'=8,'ly'=4] {'node','ly'}, dimensions={0} | all-to-all | bytes 6324224 | tf_op jit(solution)/shard_map/all_to_all | solution.py:124
  367.1 1.3 reshape.116
  368.9 2.8 fusion.9
  371.7 4.9 %pad_maximum_fusion.1 = f32[8,129,1024]{2,1,0:T(8,128)} fusion(f32[8,1,1024]{2,1,0:T(1,128)S(1)} %copy.69, f32[8,128,1024]{2,1,0:T(8,128)} %fusion.9), kind=kLoop, calls=%fused_computation.9 | loop fusion | flops 1056768 | bytes 8454144 | tf_op jit(solution)/shard_map/concatenate | solution.py:150
  376.7 30.0 %reduce-scatter.11.cloned.1.call-done = f32[1,128,1024]{2,1,0:T(8,128)} async-done(((f32[8,128,1024]{2,1,0:T(8,128)}), f32[1,128,1024]{2,1,0:T(8,128)}) %reduce-scatter.11.cloned.1.call-update) | async-done | bytes 524304 | tf_op jit(solution)/shard_map/reduce_scatter | solution.py:153
  410.2 55.5 %reduce-scatter.9.cloned.1.call-done = f32[1,129,1024]{2,1,0:T(8,128)} async-done(((f32[8,129,1024]{2,1,0:T(8,128)}), f32[1,129,1024]{2,1,0:T(8,128)}) %reduce-scatter.9.cloned.1.call-update) | async-done | bytes 528400 | tf_op jit(solution)/shard_map/reduce_scatter | solution.py:149
  (70 shorter events, 17.3 us)
Async XLA Ops:
  7.2 61.5 %all-gather.10.cloned.1.call-start = ((), (), s32[]{:S(2)}) async-start(), calls=%async_computation.14 | async-start | bytes 4718592 | tf_op jit(solution)/shard_map/all_gather | solution.py:58
  7.9 116.0 %all-gather.8.cloned.1.call-start = ((), (), s32[]{:S(2)}) async-start(), calls=%async_computation.13 | async-start | bytes 4718592 | tf_op jit(solution)/shard_map/all_gather | solution.py:59
  77.1 5.5 %copy-start.4 = (bf16[1,512,384]{2,1,0:T(8,128)(2,1)S(1)}, bf16[1,512,384]{2,1,0:T(8,128)(2,1)}, u32[]{:S(2)}) copy-start(bf16[1,512,384]{2,1,0:T(8,128)(2,1)} %param.13) | copy-start | bytes 1179652
  77.1 5.5 %copy-start.5 = (bf16[1,512,384]{2,1,0:T(8,128)(2,1)S(1)}, bf16[1,512,384]{2,1,0:T(8,128)(2,1)}, u32[]{:S(2)}) copy-start(bf16[1,512,384]{2,1,0:T(8,128)(2,1)} %param.12) | copy-start | bytes 1179652
  77.1 5.5 %copy-start.6 = (bf16[1,512,384]{2,1,0:T(8,128)(2,1)S(1)}, bf16[1,512,384]{2,1,0:T(8,128)(2,1)}, u32[]{:S(2)}) copy-start(bf16[1,512,384]{2,1,0:T(8,128)(2,1)} %param.11) | copy-start | bytes 1179652
  77.1 79.8 %all-to-all-start.1 = ((bf16[8,193,2048]{2,1,0:T(8,128)(2,1)}), bf16[8,193,2048]{2,1,0:T(8,128)(2,1)}, u32[]{:S(2)}, u32[]{:S(2)}) async-start(bf16[8,193,2048]{2,1,0:T(8,128)(2,1)} %fusion.1), calls=%async_computation.1 | async-start | bytes 13107200 | tf_op jit(solution)/shard_map/all_to_all | solution.py:106
  82.6 96.9 %all-gather.6.cloned.1.call-start = ((), (), s32[]{:S(2)}) async-start(), calls=%async_computation.8 | async-start | bytes 5898240 | tf_op jit(solution)/shard_map/all_gather | solution.py:100
  157.0 76.1 %all-to-all-start = ((bf16[8,192,2048]{2,1,0:T(8,128)(2,1)}), bf16[8,192,2048]{2,1,0:T(8,128)(2,1)}, u32[]{:S(2)}, u32[]{:S(2)}) async-start(bf16[8,192,2048]{2,1,0:T(8,128)(2,1)} %bitcast.59), calls=%async_computation | async-start | bytes 12582912 | tf_op jit(solution)/shard_map/all_to_all | solution.py:107
  161.8 209.9 %reduce-scatter.5.cloned.1.call-start = ((), (), s32[]{:S(2)}) async-start(), calls=%async_computation.9 | async-start | bytes 3932160 | tf_op jit(solution)/shard_map/reduce_scatter | solution.py:142
  179.5 7.4 %copy-start.1 = (bf16[8,192,2048]{2,1,0:T(8,128)(2,1)S(1)}, bf16[8,192,2048]{2,1,0:T(8,128)(2,1)}, u32[]{:S(2)}) copy-start(bf16[8,192,2048]{2,1,0:T(8,128)(2,1)} %slice.70) | copy-start | bytes 18874372
  242.5 129.2 %reduce-scatter.7.cloned.1.call-start = ((), (), s32[]{:S(2)}) async-start(), calls=%async_computation.10 | async-start | bytes 7864320 | tf_op jit(solution)/shard_map/reduce_scatter | solution.py:143
  251.1 5.2 %copy-start.3 = (bf16[1536,384]{0,1:T(8,128)(2,1)}, bf16[1536,384]{0,1:T(8,128)(2,1)S(1)}, u32[]{:S(2)}) copy-start(bf16[1536,384]{0,1:T(8,128)(2,1)S(1)} %get-tuple-element.42) | copy-start | bytes 3538948
  264.2 142.5 %reduce-scatter.11.cloned.1.call-start = ((), (), s32[]{:S(2)}) async-start(), calls=%async_computation.12 | async-start | bytes 4718592 | tf_op jit(solution)/shard_map/reduce_scatter | solution.py:153
  321.5 1.9 copy-start
  321.5 144.2 %reduce-scatter.9.cloned.1.call-start = ((), (), s32[]{:S(2)}) async-start(), calls=%async_computation.11 | async-start | bytes 5013504 | tf_op jit(solution)/shard_map/reduce_scatter | solution.py:149
  376.7 31.1 %copy-start.2 = (f32[512,768]{0,1:T(8,128)S(1)}, f32[512,768]{0,1:T(8,128)}, u32[]{:S(2)}) copy-start(f32[512,768]{0,1:T(8,128)} %reduce-scatter.7.cloned.1.call-done) | copy-start | bytes 4718596
Sparse Core Ops, SparseCore 0:
  9.8 58.8 all-gather.9
  70.5 53.4 all-gather.7
  125.8 53.7 all-gather.5
  242.6 37.8 reduce-scatter.4
  282.9 66.2 reduce-scatter.6
  351.6 55.0 reduce-scatter.10
  409.2 56.4 reduce-scatter.8
where the time goes:
time: 476 us; the launch traced here: 475 us
  waiting for transfers between devices  237 us (50%)
  blocking collectives  107 us (22%)
  matrix products  64.7 us (14%)
  local copies, waits for them, and re-layouts  22.2 us (5%)
  other arithmetic  19.3 us (4%)
  between operations  14.4 us (3%)
  starting transfers between devices  11.1 us (2%)
    reduce_scatter x1, waiting for transfers between devices, local(): lax.psum_scatter(jnp.concatenate([partial_lo, gate_cols], axis=1), 'lz',...  55.5 us
    all_to_all x1, blocking collectives, local(): lax.all_to_all(back_lo, ('node', 'ly'), split_axis=0, concat_axis=0, tile...  41.8 us
    all_to_all x1, blocking collectives, local(): lax.all_to_all(back_hi, ('node', 'ly'), split_axis=0, concat_axis=0, tile...  41.4 us
    all_to_all x1, waiting for transfers between devices, local(): lax.all_to_all(send_dy, ('node', 'ly'), split_axis=0, concat_axis=0, tile...  40.5 us
    all_gather x1, waiting for transfers between devices, local(): seen_dy = lax.all_gather(cotangent, 'lz', axis=0, tiled=False)  40.2 us
    all_gather x1, waiting for transfers between devices, local(): seen_x = lax.all_gather(tokens, 'lz', axis=0, tiled=False)  33.4 us
    reduce_scatter x1, waiting for transfers between devices, local(): lax.psum_scatter(partial_hi, 'lz', scatter_dimension=0, tiled=True)[0]  30 us
    all_to_all x1, waiting for transfers between devices, local(): lax.all_to_all(send_x, ('node', 'ly'), split_axis=0, concat_axis=0, tiled...  25.9 us
  transfers between devices with their start and end apart: 9, of which 7 were waited for; matrix products, arithmetic and copies ran while one was open for 19% of the time, Pallas kernels for 0%

commit v1 on v0

--- a/solution.py
+++ b/solution.py
@@ -2,6 +2,12 @@
 import jax.numpy as jnp
 from jax import lax
 from jax.sharding import PartitionSpec as P
+
+
+def tiled_gather(x, axis, dim):
+    length = lax.axis_size(axis)
+    repeats = [length if d == dim else 1 for d in range(x.ndim)]
+    return lax.all_to_all(jnp.tile(x, repeats), axis, split_axis=dim, concat_axis=dim, tiled=True)
 
 
 def expert_rows(rows_x, rows_dy, rows_gate, gate_proj, up_proj, down_proj):
@@ -97,9 +103,7 @@
         .astype(jnp.bfloat16)
         .reshape(near, planes * capacity, width)
     )
-    all_weights = lax.all_gather(
-        jnp.concatenate([w_gate, w_up, w_down], axis=2), "dp", axis=1, tiled=True
-    )[0]
+    all_weights = tiled_gather(jnp.concatenate([w_gate, w_up, w_down], axis=2), "dp", 1)[0]
     gate_proj = all_weights[:, :hidden_units]
     up_proj = all_weights[:, hidden_units : 2 * hidden_units]
     down_proj = all_weights[:, 2 * hidden_units :]

time: 476 us -> 677 us (1.42); the launches traced: 475 us -> 667 us
  local copies, waits for them, and re-layouts: 22.2 us -> 130 us
  other arithmetic: 19.3 us -> 120 us
  waiting for transfers between devices: 237 us -> 215 us
  starting transfers between devices: 11.1 us -> 19.7 us
    unnamed x0 -> x1, other arithmetic: none -> 102 us
    another operation x0 -> x2, local copies, waits for them, and re-layouts: none -> 89 us  [tiled_gather(): jnp.tile(x, repeats)]
    all_to_all x1, waiting for transfers between devices: 25.9 us -> 65.6 us  [local(): lax.all_to_all(send_x, ('node', 'ly'), split_axis=0, concat_axis=0, tiled...]
    all_gather x1, waiting for transfers between devices: 40.2 us -> 1.22 us  [local(): seen_dy = lax.all_gather(cotangent, 'lz', axis=0, tiled=False)]
    all_gather x1, waiting for transfers between devices: 33.4 us -> 0.02 us  [local(): seen_x = lax.all_gather(tokens, 'lz', axis=0, tiled=False)]
    unnamed x18 -> x22, local copies, waits for them, and re-layouts: 4.83 us -> 26.2 us
    all_to_all x0 -> x1, waiting for transfers between devices: none -> 15.9 us  [tiled_gather(): lax.all_to_all(jnp.tile(x, repeats), axis, split_axis=dim, concat_axis=di...]
    all_gather x1 -> x0, waiting for transfers between devices: 10.1 us -> none  [local(): lax.all_gather(jnp.concatenate([w_gate, w_up, w_down], axis=2), 'dp', axi...]
  transfers between devices with their start and end apart: 9 -> 9, of which waited for: 7 -> 6; matrix products, arithmetic and copies ran while one was open for 19% -> 44% of each run, Pallas kernels for 0% -> 0%
where the time goes in v1:
time: 677 us; the launch traced here: 667 us
  waiting for transfers between devices  215 us (32%)
  local copies, waits for them, and re-layouts  130 us (19%)
  other arithmetic  120 us (18%)
  blocking collectives  108 us (16%)
  matrix products  60.1 us (9%)
  starting transfers between devices  19.7 us (3%)
  between operations  14.6 us (2%)
    unnamed x1, other arithmetic  102 us
    another operation x2, local copies, waits for them, and re-layouts, tiled_gather(): jnp.tile(x, repeats)  89 us
    all_to_all x1, waiting for transfers between devices, local(): lax.all_to_all(send_x, ('node', 'ly'), split_axis=0, concat_axis=0, tiled...  65.6 us
    reduce_scatter x1, waiting for transfers between devices, local(): lax.psum_scatter(jnp.concatenate([partial_lo, gate_cols], axis=1), 'lz',...  55.4 us
    all_to_all x1, waiting for transfers between devices, local(): lax.all_to_all(send_dy, ('node', 'ly'), split_axis=0, concat_axis=0, tile...  43 us
    all_to_all x1, blocking collectives, local(): lax.all_to_all(back_lo, ('node', 'ly'), split_axis=0, concat_axis=0, tile...  41.8 us
    all_to_all x1, blocking collectives, local(): lax.all_to_all(back_hi, ('node', 'ly'), split_axis=0, concat_axis=0, tile...  40.9 us
    reduce_scatter x1, waiting for transfers between devices, local(): lax.psum_scatter(partial_hi, 'lz', scatter_dimension=0, tiled=True)[0]  32.6 us
  transfers between devices with their start and end apart: 9, of which 6 were waited for; matrix products, arithmetic and copies ran while one was open for 44% of the time, Pallas kernels for 0%

profile of v1, /device:TPU:1, one launch (start us, length us, event | category | flops | bytes accessed | tf_op | source)
XLA Modules:
  0.0 667.2 jit_solution(5116067263723619479)
XLA Ops:
  9.6 88.7 %copy.109 = bf16[1,2048,1152]{2,0,1:T(2,128)(2,1)} copy(bf16[1,2048,1152]{2,1,0:T(8,128)(2,1)S(1)} %bitcast.72) | data formatting | bytes 9437184 | tf_op jit(solution)/shard_map/tile | solution.py:10
  98.8 101.9 %reduce.11 = bf16[2048,1152]{1,0:T(8,128)(2,1)} reduce(bf16[2048,1,1152]{2,1,0:T(2,128)(2,1)} %bitcast.68, bf16[]{:T(256)} %broadcast.105), dimensions={1}, to_apply=%bitcast.67.reduce_sub_computation | reduce | bytes 9437186
  200.7 5.5 reshape.135
  206.2 5.1 all-to-all-start.2
  212.3 25.4 %all_gather.19 = bf16[8,1,2048]{2,1,0:T(2,128)(2,1)S(1)} all-gather(bf16[1,1,2048]{2,1,0:T(2,128)(2,1)S(1)} %all_gather.18), channel_id=1, replica_groups=mesh['dp'=4,'node'=2,'lz'=8,'ly'=4] {'lz'}, dimensions={0}, use_global_device_ids=true | all-gather | bytes 36864 | tf_op jit(solution)/shard_map/all_gather | solution.py:63
  239.3 4.0 convert_bitcast_fusion
  244.5 3.4 fusion.1
  247.8 15.9 %all-to-all-done.2 = bf16[4,2,294912]{2,1,0:T(2,128)(2,1)} async-done(((bf16[4,2,294912]{2,1,0:T(2,128)(2,1)}), bf16[4,2,294912]{2,1,0:T(2,128)(2,1)}, u32[]{:S(2)}, u32[]{:S(2)}) %all-to-all-start.2) | async-done | bytes 4718624 | tf_op jit(solution)/shard_map/all_to_all | solution.py:10
  263.7 8.3 %all-to-all-start.1 = ((bf16[8,193,2048]{2,1,0:T(8,128)(2,1)}), bf16[8,193,2048]{2,1,0:T(8,128)(2,1)}, u32[]{:S(2)}, u32[]{:S(2)}) async-start(bf16[8,193,2048]{2,1,0:T(8,128)(2,1)} %fusion.1), calls=%async_computation.1 | async-start | bytes 13107200 | tf_op jit(solution)/shard_map/all_to_all | solution.py:110
  273.2 4.0 convert_bitcast_fusion.1
  277.2 3.3 copy.76
  280.5 65.6 %all-to-all-done.1 = bf16[8,193,2048]{2,1,0:T(8,128)(2,1)} async-done(((bf16[8,193,2048]{2,1,0:T(8,128)(2,1)}), bf16[8,193,2048]{2,1,0:T(8,128)(2,1)}, u32[]{:S(2)}, u32[]{:S(2)}) %all-to-all-start.1) | async-done | bytes 6324256 | tf_op jit(solution)/shard_map/all_to_all | solution.py:110
  346.1 5.0 all-to-all-start
  351.4 8.1 %reshape.136 = bf16[2048,1,1152]{2,1,0:T(2,128)(2,1)} reshape(bf16[4,2,294912]{2,1,0:T(2,128)(2,1)} %all-to-all-done.2) | data formatting | bytes 9437184
  359.5 6.6 copy.108
  366.9 3.5 slice.70
  371.1 4.1 fusion.18
  375.2 4.2 fusion.22
  379.4 43.0 %all-to-all-done = bf16[8,192,2048]{2,1,0:T(8,128)(2,1)} async-done(((bf16[8,192,2048]{2,1,0:T(8,128)(2,1)}), bf16[8,192,2048]{2,1,0:T(8,128)(2,1)}, u32[]{:S(2)}, u32[]{:S(2)}) %all-to-all-start) | async-done | bytes 6291488 | tf_op jit(solution)/shard_map/all_to_all | solution.py:111
  422.4 9.4 %fusion.24 = f32[2048,384]{1,0:T(8,128)} fusion(bf16[1536,2048]{1,0:T(8,128)(2,1)} %bitcast.8, f32[1536]{0:T(1024)S(1)} %reshape.121, f32[1536,384]{0,1:T(8,128)} %fusion.18, f32[1536,384]{0,1:T(8,128)} %fusion.22), kind=kOutput, calls=%fused_computation.33 | convolution fusion | flops 2420047872 | bytes 14161920 | tf_op jit(solution)/shard_map/dot_general | solution.py:29
  432.1 8.4 %multiply_reduce_fusion = (bf16[1536]{0:T(1024)(128)(2,1)S(1)}, bf16[1536,384]{0,1:T(8,128)(2,1)S(1)}, bf16[1536,384]{0,1:T(8,128)(2,1)S(1)}) fusion(f32[1536,384]{0,1:T(8,128)} %fusion.18, f32[1536,384]{0,1:T(8,128)} %fusion.22, f32[1536]{0:T(1024)S(1)} %reshape.121, bf16[1536,2048]{1,0:T(8,128)(2,1)} %bitcast.8, bf16[2048,1152]{1,0:T(8,128)(2,1)} %bitcast.73), kind=kOutput, calls=%fused_computation.16 | convolution fusion | flops 2425944576 | bytes 14951424 | tf_op jit(solution)/shard_map/dot_general | solution.py:19
  440.5 5.2 fusion.56
  445.8 4.7 fusion.57
  450.5 3.1 pad_maximum_fusion
  454.1 4.9 fusion.20
  459.0 5.5 add_convert_fusion
  466.9 40.9 %all_to_all.25 = bf16[8,192,1024]{2,1,0:T(8,128)(2,1)S(1)} all-to-all(bf16[8,192,1024]{2,1,0:T(8,128)(2,1)S(1)} %bitcast.81), channel_id=1, replica_groups=mesh['dp'=4,'node'=2,'lz'=8,'ly'=4] {'node','ly'}, dimensions={0} | all-to-all | bytes 6291456 | tf_op jit(solution)/shard_map/all_to_all | solution.py:131
  513.0 41.8 %all_to_all.26 = bf16[8,193,1024]{2,1,0:T(8,128)(2,1)S(1)} all-to-all(bf16[8,193,1024]{2,1,0:T(8,128)(2,1)S(1)} %fusion.3), channel_id=1, replica_groups=mesh['dp'=4,'node'=2,'lz'=8,'ly'=4] {'node','ly'}, dimensions={0} | all-to-all | bytes 6324224 | tf_op jit(solution)/shard_map/all_to_all | solution.py:128
  558.2 2.8 fusion.9
  561.0 4.9 pad_maximum_fusion.1
  566.0 32.6 %reduce-scatter.11.cloned.1.call-done = f32[1,128,1024]{2,1,0:T(8,128)} async-done(((f32[8,128,1024]{2,1,0:T(8,128)}), f32[1,128,1024]{2,1,0:T(8,128)}) %reduce-scatter.11.cloned.1.call-update) | async-done | bytes 524304 | tf_op jit(solution)/shard_map/reduce_scatter | solution.py:157
  602.1 55.4 %reduce-scatter.9.cloned.1.call-done = f32[1,129,1024]{2,1,0:T(8,128)} async-done(((f32[8,129,1024]{2,1,0:T(8,128)}), f32[1,129,1024]{2,1,0:T(8,128)}) %reduce-scatter.9.cloned.1.call-update) | async-done | bytes 528400 | tf_op jit(solution)/shard_map/reduce_scatter | solution.py:153
  (76 shorter events, 27.5 us)
Async XLA Ops:
  7.2 232.2 %all-gather.7.cloned.1.call-start = ((), (), s32[]{:S(2)}) async-start(), calls=%async_computation.14 | async-start | bytes 4718592 | tf_op jit(solution)/shard_map/all_gather | solution.py:64
  206.2 5.9 copy-start.5
  206.2 5.9 copy-start.6
  206.2 57.5 %all-to-all-start.2 = ((bf16[4,2,294912]{2,1,0:T(2,128)(2,1)}), bf16[4,2,294912]{2,1,0:T(2,128)(2,1)}, u32[]{:S(2)}, u32[]{:S(2)}) async-start(bf16[4,2,294912]{2,1,0:T(2,128)(2,1)} %reshape.135), calls=%async_computation.2 | async-start | bytes 9437184 | tf_op jit(solution)/shard_map/all_to_all | solution.py:10
  211.3 61.9 %all-gather.5.cloned.1.call-start = ((), (), s32[]{:S(2)}) async-start(), calls=%async_computation.13 | async-start | bytes 4718592 | tf_op jit(solution)/shard_map/all_gather | solution.py:65
  263.7 82.4 %all-to-all-start.1 = ((bf16[8,193,2048]{2,1,0:T(8,128)(2,1)}), bf16[8,193,2048]{2,1,0:T(8,128)(2,1)}, u32[]{:S(2)}, u32[]{:S(2)}) async-start(bf16[8,193,2048]{2,1,0:T(8,128)(2,1)} %fusion.1), calls=%async_computation.1 | async-start | bytes 13107200 | tf_op jit(solution)/shard_map/all_to_all | solution.py:110
  346.1 76.3 %all-to-all-start = ((bf16[8,192,2048]{2,1,0:T(8,128)(2,1)}), bf16[8,192,2048]{2,1,0:T(8,128)(2,1)}, u32[]{:S(2)}, u32[]{:S(2)}) async-start(bf16[8,192,2048]{2,1,0:T(8,128)(2,1)} %bitcast.70), calls=%async_computation | async-start | bytes 12582912 | tf_op jit(solution)/shard_map/all_to_all | solution.py:111
  351.1 209.9 %reduce-scatter.5.cloned.1.call-start = ((), (), s32[]{:S(2)}) async-start(), calls=%async_computation.9 | async-start | bytes 3932160 | tf_op jit(solution)/shard_map/reduce_scatter | solution.py:146
  366.9 4.2 copy-start
  370.4 4.7 copy-start.2
  431.8 129.2 %reduce-scatter.7.cloned.1.call-start = ((), (), s32[]{:S(2)}) async-start(), calls=%async_computation.10 | async-start | bytes 7864320 | tf_op jit(solution)/shard_map/reduce_scatter | solution.py:147
  440.5 5.3 copy-start.4
  453.6 145.0 %reduce-scatter.11.cloned.1.call-start = ((), (), s32[]{:S(2)}) async-start(), calls=%async_computation.12 | async-start | bytes 4718592 | tf_op jit(solution)/shard_map/reduce_scatter | solution.py:157
  510.7 2.0 copy-start.1
  510.7 146.8 %reduce-scatter.9.cloned.1.call-start = ((), (), s32[]{:S(2)}) async-start(), calls=%async_computation.11 | async-start | bytes 5013504 | tf_op jit(solution)/shard_map/reduce_scatter | solution.py:153
  566.0 33.7 %copy-start.3 = (f32[512,768]{0,1:T(8,128)S(1)}, f32[512,768]{0,1:T(8,128)}, u32[]{:S(2)}) copy-start(f32[512,768]{0,1:T(8,128)} %reduce-scatter.7.cloned.1.call-done) | copy-start | bytes 4718596
Sparse Core Ops, SparseCore 0:
  9.8 58.6 all-gather.6
  213.9 59.2 all-gather.4
  431.9 40.4 reduce-scatter.4
  474.8 66.2 reduce-scatter.6
  543.5 55.0 reduce-scatter.10
  601.0 56.4 reduce-scatter.8
